TPU v7x, 32 devices: a whole 2x2x4 slice. The times are simulated.
32 devices in a mesh: rep: 4 (over x, core), frame: 4 (over z), row: 2 (over y).
Axes of the slice: x: 2, y: 2, z: 4, core: 2. Of those that a mesh axis runs over, the one named last changes fastest.
Arguments:
- activations: bfloat16 [4, 4, 16, 32, 1280], P('rep', 'frame', 'row'), may hold values from -70 to 70, as said below
- spatial_weight: bfloat16 [9, 1280, 1280], P(None, None, ('rep', 'frame')), may hold values from -0.0546875 to 0.0546875
- temporal_weight: bfloat16 [3, 1280, 1280], P(None, None, ('rep', 'frame')), may hold values from -0.09375 to 0.09375
- first_gain: float32 [1280], replicated, may hold values from 0.25 to 1.75
- first_shift: float32 [1280], replicated, may hold values from -1.5 to 1.5
- spatial_bias: float32 [1280], replicated, may hold values from -2.5 to 2.5
- second_gain: float32 [1280], replicated, may hold values from 0.25 to 1.75
- second_shift: float32 [1280], replicated, may hold values from -1.5 to 1.5
- temporal_bias: float32 [1280], replicated, may hold values from -1.5 to 1.5
Outputs:
- block_out: float32 [4, 4, 16, 32, 1280], P('rep', 'frame', 'row')
Inputs may be any that keep to these rules, and one draw needn't show every extreme that they name: `activations`: finite values.
All inputs are finite; a program needn't handle non-finite values.
Results may differ from a plain program's by a relative error of at most 0.0009.
Values may be sent and summed in bfloat16 or wider, within the bound.
No kernel may reach another device: no remote copies, remote signals or barrier semaphores. Data moves between devices by JAX's collectives and lax.ppermute only.
A program may use at most 128 MiB of HBM per device.

v0:
```python
import numpy as np
import jax
import jax.numpy as jnp
from jax import lax
from jax.sharding import PartitionSpec as P

GROUPS = 32
EPS = 1e-05


def pair_sum(value, axis):
    if lax.axis_size(axis) == 2:
        return jax.tree.map(lambda v: v + lax.ppermute(v, axis, [(0, 1), (1, 0)]), value)
    return lax.psum(value, axis)


def gather_rep(w):
    size = lax.axis_size("rep")
    if size & size - 1 != 0:
        return (lax.all_gather(w, "rep", axis=w.ndim - 1, tiled=True), list(range(size)))
    index = lax.axis_index("rep")
    blocks = w[None]
    order = [0]
    step = size // 2
    while step >= 1:
        recv = lax.ppermute(blocks, "rep", [(k, k ^ step) for k in range(size)])
        upper = index & step != 0
        low = jnp.where(upper, recv, blocks)
        high = jnp.where(upper, blocks, recv)
        blocks = jnp.concatenate([low, high], axis=0)
        order = order + [o + step for o in order]
        step //= 2
    out = jnp.moveaxis(blocks, 0, -2)
    return (out.reshape(out.shape[:-2] + (-1,)), order)


def local_vector(vec, order, frame_index, rep_size, frame_size):
    width = vec.shape[0] // (rep_size * frame_size)
    table = vec.reshape(rep_size, frame_size, width)[np.array(order)]
    return lax.dynamic_index_in_dim(table, frame_index, axis=1, keepdims=False).reshape(-1)


def silu_bf16(normed):
    return jax.nn.silu(normed).astype(jnp.bfloat16)


def shards(
    activations,
    spatial_weight,
    temporal_weight,
    first_gain,
    first_shift,
    spatial_bias,
    second_gain,
    second_shift,
    temporal_bias,
):
    rep_size = lax.axis_size("rep")
    frame_size = lax.axis_size("frame")
    row_size = lax.axis_size("row")
    frame_index = lax.axis_index("frame")
    row_index = lax.axis_index("row")
    channels = activations.shape[-1]
    rows = activations.shape[2]
    cols = activations.shape[3]
    width = channels // GROUPS
    shard_width = spatial_weight.shape[-1]
    spatial_w, order = gather_rep(spatial_weight)
    temporal_w, _ = gather_rep(temporal_weight)
    local = spatial_w.shape[-1]
    raw = lax.all_gather(activations, "frame", axis=1, tiled=True)
    frames = raw.shape[1]
    if row_size > 1:
        down = [(i, i + 1) for i in range(row_size - 1)]
        up = [(i + 1, i) for i in range(row_size - 1)]
        above = lax.ppermute(raw[:, :, rows - 1 :], "row", down)
        below = lax.ppermute(raw[:, :, :1], "row", up)
    else:
        above = jnp.zeros_like(raw[:, :, :1])
        below = jnp.zeros_like(raw[:, :, :1])
    inputs = raw.astype(jnp.float32)
    grouped = inputs.reshape(1, -1, GROUPS, width)
    sums = jnp.sum(grouped, axis=(1, 3))
    squares = jnp.sum(grouped * grouped, axis=(1, 3))
    sums, squares = pair_sum((sums, squares), "row")
    count = grouped.shape[1] * width * row_size
    mean = sums / count
    variance = squares / count - mean * mean
    inverse = lax.rsqrt(variance + EPS)
    mean_full = jnp.repeat(mean, width, axis=1)[:, None, None, None, :]
    inverse_full = jnp.repeat(inverse, width, axis=1)[:, None, None, None, :]

    def first_norm(x):
        normed = (x.astype(jnp.float32) - mean_full) * inverse_full * first_gain + first_shift
        return silu_bf16(normed)

    first_mid = first_norm(raw)
    first_above = jnp.where(row_index > 0, first_norm(above), jnp.zeros((), jnp.bfloat16))
    first_below = jnp.where(
        row_index < row_size - 1, first_norm(below), jnp.zeros((), jnp.bfloat16)
    )
    padded = jnp.concatenate([first_above, first_mid, first_below], axis=2)
    lhs = padded.reshape(frames, rows + 2, cols, channels)
    kernel = spatial_w.reshape(3, 3, channels, local)
    spatial = lax.conv_general_dilated(
        lhs,
        kernel,
        window_strides=(1, 1),
        padding=((0, 0), (1, 1)),
        dimension_numbers=("NHWC", "HWIO", "NHWC"),
        preferred_element_type=jnp.float32,
    )
    spatial = spatial + local_vector(spatial_bias, order, frame_index, rep_size, frame_size)
    g2 = local_vector(second_gain, order, frame_index, rep_size, frame_size)
    s2 = local_vector(second_shift, order, frame_index, rep_size, frame_size)
    if shard_width % width == 0:
        grouped2 = spatial.reshape(-1, local // width, width)
        sums2 = jnp.sum(grouped2, axis=(0, 2))
        squares2 = jnp.sum(grouped2 * grouped2, axis=(0, 2))
        sums2, squares2 = pair_sum((sums2, squares2), "row")
        count2 = grouped2.shape[0] * width * row_size
        mean2 = sums2 / count2
        variance2 = squares2 / count2 - mean2 * mean2
        inverse2 = lax.rsqrt(variance2 + EPS)
        mean2_full = jnp.repeat(mean2, width)
        inverse2_full = jnp.repeat(inverse2, width)
    else:
        flat = spatial.reshape(-1, local)
        csum = jnp.sum(flat, axis=0)
        csq = jnp.sum(flat * flat, axis=0)
        csum, csq = pair_sum((csum, csq), "row")
        both = lax.all_gather(jnp.stack([csum, csq]), "frame", axis=0)
        both = both.reshape(frame_size, 2, rep_size, shard_width)
        inv_order = np.argsort(np.array(order))
        both = both[:, :, inv_order]
        both = jnp.transpose(both, (1, 2, 0, 3)).reshape(2, GROUPS, -1)
        gsum = jnp.sum(both, axis=2)
        count2 = flat.shape[0] * row_size * width
        gmean = gsum[0] / count2
        gvar = gsum[1] / count2 - gmean * gmean
        ginv = lax.rsqrt(gvar + EPS)
        mean2_full = local_vector(
            jnp.repeat(gmean, width), order, frame_index, rep_size, frame_size
        )
        inverse2_full = local_vector(
            jnp.repeat(ginv, width), order, frame_index, rep_size, frame_size
        )
    second = silu_bf16((spatial - mean2_full) * inverse2_full * g2 + s2)
    second_all = lax.all_gather(second, "frame", axis=3, tiled=True)
    rows_order = np.arange(channels).reshape(rep_size, frame_size, shard_width)
    rows_order = rows_order[np.array(order)].transpose(1, 0, 2).reshape(-1)
    temporal_w = temporal_w[:, rows_order, :]
    lhs_t = second_all.reshape(frames, rows * cols, frame_size * local)[None]
    kernel_t = temporal_w.reshape(3, 1, frame_size * local, local)
    temporal = lax.conv_general_dilated(
        lhs_t,
        kernel_t,
        window_strides=(1, 1),
        padding=((1, 1), (0, 0)),
        dimension_numbers=("NHWC", "HWIO", "NHWC"),
        preferred_element_type=jnp.float32,
    )
    temporal = temporal.reshape(1, frames, rows, cols, local).astype(jnp.bfloat16)
    back = lax.all_to_all(temporal, "frame", split_axis=1, concat_axis=4, tiled=True)
    per_frame = frames // frame_size
    back = back.reshape(1, per_frame, rows, cols, frame_size, rep_size, shard_width)
    back = back[:, :, :, :, :, np.argsort(np.array(order))]
    back = jnp.swapaxes(back, 4, 5).reshape(1, per_frame, rows, cols, channels)
    return activations.astype(jnp.float32) + back.astype(jnp.float32) + temporal_bias


def solution(mesh):
    placed = (
        P("rep", "frame", "row", None, None),
        P(None, None, ("rep", "frame")),
        P(None, None, ("rep", "frame")),
        P(),
        P(),
        P(),
        P(),
        P(),
        P(),
    )
    return jax.shard_map(
        shards,
        mesh=mesh,
        in_specs=placed,
        out_specs=P("rep", "frame", "row", None, None),
        check_vma=False,
    )
```

profile of v0, /device:TPU:0, one launch (start us, length us, event | category | flops | bytes accessed | tf_op | source)
XLA Modules:
  0.0 381.3 jit_solution(2174034292066160613)
XLA Ops:
  6.5 0.7 all-gather.3.cloned.1.call-update
  7.3 3.0 collective-permute-start.4
  10.3 0.8 reshape.102
  11.1 0.7 pad_clamp_fusion.1
  11.8 0.6 gather_fusion
  12.4 0.1 add.127
  12.5 0.8 reshape.104
  13.2 0.6 gather_fusion.2
  13.8 0.8 reshape.103
  14.6 0.6 gather_fusion.1
  15.2 0.1 add.135
  15.4 35.5 %collective-permute-done.4 = bf16[1,9,1280,80]{2,3,1,0:T(8,128)(2,1)} collective-permute-done((bf16[1,9,1280,80]{2,3,1,0:T(8,128)(2,1)}, bf16[1,9,1280,80]{2,3,1,0:T(8,128)(2,1)}, u32[]{:S(2)}, u32[]{:S(2)}) %collective-permute-start.4) | collective-permute-done | bytes 1843232 | tf_op jit(solution)/shard_map/ppermute | solution.py:26
  50.8 2.3 broadcast_select_fusion.3
  53.2 2.4 pad_maximum_fusion
  55.6 10.8 %all-gather.3.cloned.1.call-done = bf16[1,4,8,32,1280]{4,3,2,0,1:T(8,128)(2,1)} async-done(((bf16[1,1,8,32,1280]{4,3,2,0,1:T(8,128)(2,1)}), bf16[1,4,8,32,1280]{4,3,2,0,1:T(8,128)(2,1)}) %all-gather.3.cloned.1.call-update) | async-done | bytes 2621456 | tf_op jit(solution)/shard_map/all_gather | solution.py:71
  66.4 1.1 fusion.28
  67.5 3.4 collective-permute-start
  70.9 2.5 convert_reduce_fusion
  73.5 0.1 reduce_sum.53
  73.8 0.1 reduce_sum.57
  73.9 2.1 collective-permute-start.2
  76.0 1.3 collective-permute-start.3
  77.3 0.5 collective-permute-done.1
  77.8 0.1 broadcast_in_dim.52
  78.1 3.5 fusion.14
  81.7 4.6 %collective-permute-done.3 = bf16[1,4,1,32,1280]{4,3,2,0,1:T(8,128)(2,1)S(1)} collective-permute-done((bf16[1,4,1,32,1280]{4,3,2,0,1:T(8,128)(2,1)S(1)}, bf16[1,4,1,32,1280]{4,3,2,0,1:T(8,128)(2,1)S(1)}, u32[]{:S(2)}, u32[]{:S(2)}) %collective-permute-start.3) | collective-permute-done | bytes 327712 | tf_op jit(solution)/shard_map/ppermute | solution.py:77
  86.3 0.5 fusion.25
  86.8 0.4 maximum_bitcast_fusion.1
  87.2 2.5 copy.78
  89.7 1.6 pad.clone
  91.4 0.5 slice.23
  91.9 4.8 %fusion.1 = bf16[10,4,8,7,1280]{4,1,3,2,0:T(4,128)(2,1)} fusion(bf16[10,4,7,2,1280]{4,1,3,2,0:T(4,128)(2,1)S(1)} %slice.23, bf16[10,4,8,5,1280]{4,1,3,2,0:T(4,128)(2,1)S(1)} %bitcast.63), kind=kLoop, calls=%fused_computation.11 | loop fusion | flops 17203200 | bytes 11264000 | tf_op jit(solution)/shard_map/conv_general_dilated | solution.py:105
  96.7 4.7 %broadcast_select_fusion.1 = (bf16[2,9,1280,80]{2,3,1,0:T(8,128)(2,1)}, bf16[2,9,1280,80]{2,3,1,0:T(8,128)(2,1)}) fusion(bf16[2,9,1280,80]{2,3,1,0:T(8,128)(2,1)} %collective-permute-done.5, pred[]{:T(512)S(6)} %ne.8, bf16[1,9,1280,80]{2,3,1,0:T(8,128)(2,1)S(1)} %copy-done.1, bf16[1,9,1280,80]{2,3,1,0:T(8,128)(2,1)S(1)} %get-tuple-element.13), kind=kLoop, calls=%fused_computation.27 | loop fusion | flops 5529600 | bytes 14745601 | tf_op jit(solution)/shard_map/jit(_where)/select_n | solution.py:28
  101.5 6.8 %maximum_bitcast_fusion = bf16[9,1280,4,80]{1,3,0,2:T(8,128)(2,1)} fusion(bf16[2,9,1280,80]{2,3,1,0:T(8,128)(2,1)} %get-tuple-element.12, bf16[2,9,1280,80]{2,3,1,0:T(8,128)(2,1)} %get-tuple-element.11), kind=kLoop, calls=%fused_computation.10 | loop fusion | flops 3686400 | bytes 14745600 | tf_op jit(solution)/shard_map/transpose | solution.py:33
  108.2 3.8 copy.66
  112.0 17.7 %select_reduce_fusion = (f32[320]{0:T(512)S(1)}, f32[320]{0:T(512)S(1)}, f32[8,32,5,320]{3,1,2,0:T(8,128)S(1)}) fusion(pred[32,5]{0,1:T(8,128)(4,1)S(1)} %copy-done.7, f32[320]{0:T(512)S(1)} %add.127, bf16[3,3,1280,320]{2,3,1,0:T(8,128)(2,1)S(1)} %bitcast.65, bf16[10,4,8,7,1280]{4,1,3,2,0:T(4,128)(2,1)} %fusion.1), kind=kOutput, calls=%fused_computation.34 | convolution fusion | flops 9440051200 | bytes 14749600 | tf_op jit(solution)/shard_map/conv_general_dilated | solution.py:105
  129.8 0.1 reduce_sum.81
  130.1 0.1 reduce_sum.78
  130.2 2.1 collective-permute-start.6
  132.3 1.3 collective-permute-done.7
  133.6 0.3 collective-permute-done.6
  134.2 0.6 multiply_convert_fusion
  134.8 0.3 copy.67
  135.2 5.4 %copy.68 = bf16[4,8,32,320]{2,1,0,3:T(8,128)(2,1)} copy(bf16[4,8,32,320]{3,1,2,0:T(8,128)(2,1)S(1)} %slice_bitcast_fusion) | data formatting | bytes 1310720 | tf_op jit(solution)/shard_map/convert_element_type | solution.py:44
  140.7 1.5 collective-permute-start.8
  142.3 11.1 %collective-permute-done.8 = bf16[1,3,1280,80]{2,3,0,1:T(8,128)(2,1)S(1)} collective-permute-done((bf16[1,3,1280,80]{2,3,0,1:T(8,128)(2,1)S(1)}, bf16[1,3,1280,80]{2,3,0,1:T(8,128)(2,1)S(1)}, u32[]{:S(2)}, u32[]{:S(2)}) %collective-permute-start.8) | collective-permute-done | bytes 614432 | tf_op jit(solution)/shard_map/ppermute | solution.py:26
  153.4 0.1 broadcast_select_fusion.7
  153.5 0.1 pad_maximum_fusion.2
  153.7 2.9 collective-permute-done.9
  156.6 0.2 broadcast_select_fusion.5
  156.8 0.2 pad_maximum_fusion.1
  157.0 6.3 %copy.69 = bf16[3,1280,320]{2,0,1:T(4,128)(2,1)} copy(bf16[3,1280,320]{1,2,0:T(8,128)(2,1)S(1)} %bitcast.64) | data formatting | bytes 4915200 | tf_op jit(solution)/shard_map/reshape | solution.py:34
  163.3 12.0 %gather_fusion.3 = bf16[1280,3,320]{2,1,0:T(4,128)(2,1)} fusion(bf16[3,1280,320]{2,0,1:T(4,128)(2,1)} %copy.69, s32[2048]{0:T(1024)S(1)} %pad_clamp_fusion), kind=kCustom, calls=%fused_computation.3 | custom fusion | bytes 4920320 | tf_op jit(solution)/shard_map/gather | solution.py:152
  175.4 148.9 %all-gather.5.cloned.1.call-done = bf16[4,8,32,1280]{2,1,0,3:T(8,128)(2,1)} async-done(((bf16[4,8,32,320]{2,1,0,3:T(8,128)(2,1)}), bf16[4,8,32,1280]{2,1,0,3:T(8,128)(2,1)}) %all-gather.5.cloned.1.call-update) | async-done | bytes 2621456 | tf_op jit(solution)/shard_map/all_gather | solution.py:149
  324.3 12.8 %copy.70 = bf16[4,8,32,1280]{3,1,2,0:T(8,128)(2,1)S(1)} copy(bf16[4,8,32,1280]{2,1,0,3:T(8,128)(2,1)} %all-gather.5.cloned.1.call-done) | data formatting | bytes 5242880 | tf_op jit(solution)/shard_map/all_gather | solution.py:149
  337.1 6.3 %fusion.22 = bf16[1,4,8,32,320]{4,2,3,0,1:T(8,128)(2,1)S(1)} fusion(bf16[4,8,32,1280]{3,1,2,0:T(8,128)(2,1)S(1)} %copy.70, bf16[3,1,1280,320]{3,0,2,1:T(4,128)(2,1)} %bitcast.69), kind=kOutput, calls=%fused_computation.41 | convolution fusion | flops 2097479680 | bytes 5734400 | tf_op jit(solution)/shard_map/conv_general_dilated | solution.py:155
  343.5 23.0 %all_to_all.15 = bf16[1,4,8,32,320]{4,2,3,0,1:T(8,128)(2,1)S(1)} all-to-all(bf16[1,4,8,32,320]{4,2,3,0,1:T(8,128)(2,1)S(1)} %fusion.22), channel_id=1, replica_groups=mesh['rep'=4,'frame'=4,'row'=2] {'frame'}, dimensions={1} | all-to-all | bytes 1310720 | tf_op jit(solution)/shard_map/all_to_all | solution.py:164
  366.4 0.6 reshape.187
  367.1 0.4 copy.74
  367.5 0.8 gather_fusion.4
  368.3 0.3 convert_bitcast_fusion
  368.5 1.4 copy.75
  369.9 2.2 reshape.124
  372.2 2.3 add_add_fusion
  (44 shorter events, 1.4 us)
Async XLA Ops:
  6.5 59.9 %all-gather.3.cloned.1.call-start = ((), (), s32[]{:S(2)}) async-start(), calls=%async_computation.1 | async-start | bytes 3276800 | tf_op jit(solution)/shard_map/all_gather | solution.py:71
  7.3 317.0 %all-gather.5.cloned.1.call-start = ((), (), s32[]{:S(2)}) async-start(), calls=%async_computation.2 | async-start | bytes 13107200 | tf_op jit(solution)/shard_map/all_gather | solution.py:149
  7.3 43.5 %collective-permute-start.4 = (bf16[1,9,1280,80]{2,3,1,0:T(8,128)(2,1)}, bf16[1,9,1280,80]{2,3,1,0:T(8,128)(2,1)}, u32[]{:S(2)}, u32[]{:S(2)}) collective-permute-start(bf16[1,9,1280,80]{2,3,1,0:T(8,128)(2,1)} %bitcast.70), channel_id=1, source_target_pairs={{0,16},{8,24},{16,0},{24,8},{1,17},{9,25},{17,1},{25,9},{2,18},{10... | collective-permute-start | bytes 5529608 | tf_op jit(solution)/shard_map/ppermute | solution.py:26
  53.1 2.4 copy-start
  55.6 22.5 %copy-start.3 = (f32[1280]{0:T(1024)S(1)}, f32[1280]{0:T(1024)}, u32[]{:S(2)}) copy-start(f32[1280]{0:T(1024)} %param.23) | copy-start | bytes 15364
  55.6 22.5 %copy-start.4 = (f32[1280]{0:T(1024)S(1)}, f32[1280]{0:T(1024)}, u32[]{:S(2)}) copy-start(f32[1280]{0:T(1024)} %param.22) | copy-start | bytes 15364
  55.6 41.2 %collective-permute-start.5 = (bf16[2,9,1280,80]{2,3,1,0:T(8,128)(2,1)}, bf16[2,9,1280,80]{2,3,1,0:T(8,128)(2,1)}, u32[]{:S(2)}, u32[]{:S(2)}) collective-permute-start(bf16[2,9,1280,80]{2,3,1,0:T(8,128)(2,1)} %pad_maximum_fusion), channel_id=1, source_target_pairs={{0,8},{8,0},{16,24},{24,16},{1,9},{9,1},{17,25},{25,17},{2,10},{10... | collective-permute-start | bytes 11059208 | tf_op jit(solution)/shard_map/ppermute | solution.py:26
  67.5 14.1 %collective-permute-start = (bf16[1,4,1,32,1280]{4,3,2,0,1:T(8,128)(2,1)S(1)}, bf16[1,4,1,32,1280]{4,3,2,0,1:T(8,128)(2,1)S(1)}, u32[]{:S(2)}, u32[]{:S(2)}) collective-permute-start(bf16[1,4,1,32,1280]{4,3,2,0,1:T(8,128)(2,1)S(1)} %get-tuple-element.15), channel_id=1, source_target_pairs={{0,1},{2,3},{4,5},{6,7},{8,9},{10,11},{12,13},{14,15},{16,17},{18,... | collective-permute-start | bytes 983048 | tf_op jit(solution)/shard_map/ppermute | solution.py:76
  73.6 4.1 %collective-permute-start.1 = (f32[1,32]{1,0:T(1,128)S(1)}, f32[1,32]{1,0:T(1,128)S(1)}, u32[]{:S(2)}, u32[]{:S(2)}) collective-permute-start(f32[1,32]{1,0:T(1,128)S(1)} %bitcast.72), channel_id=1, source_target_pairs={{0,1},{1,0},{2,3},{3,2},{4,5},{5,4},{6,7},{7,6},{8,9},{9,8},{10,11... | collective-permute-start | bytes 392 | tf_op jit(solution)/shard_map/ppermute | solution.py:13
  73.9 3.9 %collective-permute-start.2 = (f32[1,32]{1,0:T(1,128)S(1)}, f32[1,32]{1,0:T(1,128)S(1)}, u32[]{:S(2)}, u32[]{:S(2)}) collective-permute-start(f32[1,32]{1,0:T(1,128)S(1)} %bitcast.73), channel_id=1, source_target_pairs={{0,1},{1,0},{2,3},{3,2},{4,5},{5,4},{6,7},{7,6},{8,9},{9,8},{10,11... | collective-permute-start | bytes 392 | tf_op jit(solution)/shard_map/ppermute | solution.py:13
  76.0 10.3 %collective-permute-start.3 = (bf16[1,4,1,32,1280]{4,3,2,0,1:T(8,128)(2,1)S(1)}, bf16[1,4,1,32,1280]{4,3,2,0,1:T(8,128)(2,1)S(1)}, u32[]{:S(2)}, u32[]{:S(2)}) collective-permute-start(bf16[1,4,1,32,1280]{4,3,2,0,1:T(8,128)(2,1)S(1)} %get-tuple-element.16), channel_id=1, source_target_pairs={{1,0},{3,2},{5,4},{7,6},{9,8},{11,10},{13,12},{15,14},{17,16},{19,... | collective-permute-start | bytes 983048 | tf_op jit(solution)/shard_map/ppermute | solution.py:77
  91.9 4.8 %copy-start.1 = (bf16[1,9,1280,80]{2,3,1,0:T(8,128)(2,1)S(1)}, bf16[1,9,1280,80]{2,3,1,0:T(8,128)(2,1)}, u32[]{:S(2)}) copy-start(bf16[1,9,1280,80]{2,3,1,0:T(8,128)(2,1)} %copy-done) | copy-start | bytes 5529604
  108.2 3.8 copy-start.7
  129.9 3.6 collective-permute-start.7
  130.2 3.6 collective-permute-start.6
  135.2 5.5 %copy-start.2 = (bf16[3,1280,80]{1,2,0:T(8,128)(2,1)S(1)}, bf16[3,1280,80]{1,2,0:T(8,128)(2,1)}, u32[]{:S(2)}) copy-start(bf16[3,1280,80]{1,2,0:T(8,128)(2,1)} %param.21) | copy-start | bytes 1843204
  140.7 13.0 %copy-start.6 = (s32[1280]{0:T(1024)S(1)}, s32[1280]{0:T(1024)}, u32[]{:S(2)}) copy-start(s32[1280]{0:T(1024)} %constant.82) | copy-start | bytes 15364
  140.7 12.6 %collective-permute-start.8 = (bf16[1,3,1280,80]{2,3,0,1:T(8,128)(2,1)S(1)}, bf16[1,3,1280,80]{2,3,0,1:T(8,128)(2,1)S(1)}, u32[]{:S(2)}, u32[]{:S(2)}) collective-permute-start(bf16[1,3,1280,80]{2,3,0,1:T(8,128)(2,1)S(1)} %bitcast.71), channel_id=1, source_target_pairs={{0,16},{8,24},{16,0},{24,8},{1,17},{9,25},{17,1},{25,9},{2,18},{10... | collective-permute-start | bytes 1843208 | tf_op jit(solution)/shard_map/ppermute | solution.py:26
  153.6 3.0 collective-permute-start.9
  369.9 2.3 copy-start.5
Sparse Core Ops, SparseCore 0:
  8.9 57.4 all-gather.2
  140.8 183.4 all-gather.4
where the time goes:
time: 382 us; the launch traced here: 381 us
  waiting for transfers between devices  217 us (57%)
  local copies, waits for them, and re-layouts  57.4 us (15%)
  other arithmetic  32.9 us (9%)
  matrix products  24 us (6%)
  blocking collectives  23 us (6%)
  between operations  13.7 us (4%)
  starting transfers between devices  13.6 us (4%)
    all_gather x1, waiting for transfers between devices, shards(): second_all = lax.all_gather(second, 'frame', axis=3, tiled=True)  149 us
    ppermute x4, waiting for transfers between devices, gather_rep(): recv = lax.ppermute(blocks, 'rep', [(k, k ^ step) for k in range(size)])  49.5 us
    all_to_all x1, blocking collectives, shards(): lax.all_to_all(temporal, 'frame', split_axis=1, concat_axis=4, tiled=True)  23 us
    conv_general_dilated x1, matrix products, shards(): lax.conv_general_dilated(lhs, kernel, window_strides=(1, 1), padding=((0,...  17.7 us
    all_gather x1, local copies, waits for them, and re-layouts, shards(): second_all = lax.all_gather(second, 'frame', axis=3, tiled=True)  12.8 us
    gather x1, local copies, waits for them, and re-layouts, shards(): temporal_w = temporal_w[:, rows_order, :]  12 us
    all_gather x1, waiting for transfers between devices, shards(): raw = lax.all_gather(activations, 'frame', axis=1, tiled=True)  10.8 us
  transfers between devices with their start and end apart: 12, of which 9 were waited for; matrix products, arithmetic and copies ran while one was open for 12% of the time, Pallas kernels for 0%

commit v1 on v0

--- a/solution.py
+++ b/solution.py
@@ -146,7 +146,15 @@
             jnp.repeat(ginv, width), order, frame_index, rep_size, frame_size
         )
     second = silu_bf16((spatial - mean2_full) * inverse2_full * g2 + s2)
-    second_all = lax.all_gather(second, "frame", axis=3, tiled=True)
+    ways, here = (lax.axis_size("frame"), lax.axis_index("frame"))
+    grown, reach = (second, 1)
+    while reach < ways:
+        theirs = lax.ppermute(grown, "frame", [(d, d ^ reach) for d in range(ways)])
+        mine_first = jnp.concatenate([grown, theirs], axis=3)
+        theirs_first = jnp.concatenate([theirs, grown], axis=3)
+        grown = jnp.where(here & reach == 0, mine_first, theirs_first)
+        reach = 2 * reach
+    second_all = grown
     rows_order = np.arange(channels).reshape(rep_size, frame_size, shard_width)
     rows_order = rows_order[np.array(order)].transpose(1, 0, 2).reshape(-1)
     temporal_w = temporal_w[:, rows_order, :]

time: 382 us -> 268 us (0.70)
  waiting for transfers between devices: 217 us -> 104 us
  local copies, waits for them, and re-layouts: 57.4 us -> 42.2 us
  other arithmetic: 32.9 us -> 42.7 us
    all_gather x1 -> x0, waiting for transfers between devices: 149 us -> none  [shards(): second_all = lax.all_gather(second, 'frame', axis=3, tiled=True)]
    ppermute x0 -> x2, waiting for transfers between devices: none -> 47.4 us  [shards(): theirs = lax.ppermute(grown, 'frame', [(d, d ^ reach) for d in range(ways)])]
    all_gather x1 -> x0, local copies, waits for them, and re-layouts: 12.8 us -> none  [shards(): second_all = lax.all_gather(second, 'frame', axis=3, tiled=True)]
    all_gather x1, waiting for transfers between devices: 10.8 us -> 0.01 us  [shards(): raw = lax.all_gather(activations, 'frame', axis=1, tiled=True)]
    convert_element_type x3, local copies, waits for them, and re-layouts: 5.86 us -> 0.52 us  [silu_bf16(): return jax.nn.silu(normed).astype(jnp.bfloat16)]
    ppermute x0 -> x2, starting transfers between devices: none -> 4.23 us  [shards(): theirs = lax.ppermute(grown, 'frame', [(d, d ^ reach) for d in range(ways)])]
  transfers between devices with their start and end apart: 12 -> 13, of which waited for: 9 -> 7; matrix products, arithmetic and copies ran while one was open for 12% -> 34% of each run, Pallas kernels for 0% -> 0%
where the time goes in v1:
time: 268 us; the launch traced here: 267 us
  waiting for transfers between devices  104 us (39%)
  other arithmetic  42.7 us (16%)
  local copies, waits for them, and re-layouts  42.2 us (16%)
  blocking collectives  24.8 us (9%)
  matrix products  23 us (9%)
  starting transfers between devices  17.1 us (6%)
  between operations  13.8 us (5%)
    ppermute x4, waiting for transfers between devices, gather_rep(): recv = lax.ppermute(blocks, 'rep', [(k, k ^ step) for k in range(size)])  48.5 us
    ppermute x2, waiting for transfers between devices, shards(): theirs = lax.ppermute(grown, 'frame', [(d, d ^ reach) for d in range(ways)])  47.4 us
    all_to_all x1, blocking collectives, shards(): lax.all_to_all(temporal, 'frame', split_axis=1, concat_axis=4, tiled=True)  24.8 us
    conv_general_dilated x1, matrix products, shards(): lax.conv_general_dilated(lhs, kernel, window_strides=(1, 1), padding=((0,...  18.7 us
    gather x1, local copies, waits for them, and re-layouts, shards(): temporal_w = temporal_w[:, rows_order, :]  12 us
    select_n x4, other arithmetic, gather_rep(): low = jnp.where(upper, recv, blocks)  9.59 us
    transpose x1, other arithmetic, gather_rep(): out = jnp.moveaxis(blocks, 0, -2)  6.76 us
    reshape x1, local copies, waits for them, and re-layouts, gather_rep(): return (out.reshape(out.shape[:-2] + (-1,)), order)  6.23 us
  transfers between devices with their start and end apart: 13, of which 7 were waited for; matrix products, arithmetic and copies ran while one was open for 34% of the time, Pallas kernels for 0%

profile of v1, /device:TPU:0, one launch (start us, length us, event | category | flops | bytes accessed | tf_op | source)
XLA Modules:
  0.0 267.4 jit_solution(8811642105668890717)
XLA Ops:
  6.5 0.7 all-gather.2.cloned.1.call-update
  7.3 3.0 %collective-permute-start.4 = (bf16[1,9,1280,80]{2,3,1,0:T(8,128)(2,1)}, bf16[1,9,1280,80]{2,3,1,0:T(8,128)(2,1)}, u32[]{:S(2)}, u32[]{:S(2)}) collective-permute-start(bf16[1,9,1280,80]{2,3,1,0:T(8,128)(2,1)} %bitcast.79), channel_id=1, source_target_pairs={{0,16},{8,24},{16,0},{24,8},{1,17},{9,25},{17,1},{25,9},{2,18},{10... | collective-permute-start | bytes 5529608 | tf_op jit(solution)/shard_map/ppermute | solution.py:26
  10.4 0.8 reshape.213
  11.1 0.7 pad_clamp_fusion.1
  11.8 0.6 gather_fusion
  12.5 0.8 reshape.214
  13.3 0.6 gather_fusion.1
  13.8 0.8 reshape.215
  14.6 0.6 gather_fusion.2
  15.4 48.5 %collective-permute-done.10 = bf16[1,3,1280,80]{2,3,0,1:T(8,128)(2,1)S(1)} collective-permute-done((bf16[1,3,1280,80]{2,3,0,1:T(8,128)(2,1)}, bf16[1,3,1280,80]{2,3,0,1:T(8,128)(2,1)S(1)}, u32[]{:S(2)}, u32[]{:S(2)}) %collective-permute-start.10) | collective-permute-done | bytes 614432 | tf_op jit(solution)/shard_map/ppermute | solution.py:26
  63.9 1.2 broadcast_select_fusion.7
  65.0 1.3 pad_maximum_fusion.2
  66.3 2.3 broadcast_select_fusion.3
  68.6 2.3 pad_maximum_fusion
  71.0 0.5 collective-permute-start.5
  71.5 2.5 convert_reduce_fusion
  74.1 0.1 reduce_sum.53
  74.2 1.8 collective-permute-start.1
  76.2 0.3 collective-permute-start.2
  76.6 1.1 fusion.34
  77.7 3.7 %collective-permute-start = (bf16[1,4,1,32,1280]{4,3,2,0,1:T(8,128)(2,1)S(1)}, bf16[1,4,1,32,1280]{4,3,2,0,1:T(8,128)(2,1)S(1)}, u32[]{:S(2)}, u32[]{:S(2)}) collective-permute-start(bf16[1,4,1,32,1280]{4,3,2,0,1:T(8,128)(2,1)S(1)} %get-tuple-element.15), channel_id=1, source_target_pairs={{0,1},{2,3},{4,5},{6,7},{8,9},{10,11},{12,13},{14,15},{16,17},{18,... | collective-permute-start | bytes 983048 | tf_op jit(solution)/shard_map/ppermute | solution.py:76
  81.4 1.3 collective-permute-start.3
  83.1 3.5 %fusion.14 = bf16[1,4,8,32,1280]{4,3,2,0,1:T(8,128)(2,1)S(1)} fusion(bf16[1,4,8,32,1280]{4,3,2,0,1:T(8,128)(2,1)} %all-gather.2.cloned.1.call-done, f32[1280]{0:T(1024)S(1)} %copy-done.7, f32[1280]{0:T(1024)S(1)} %copy-done.8, f32[1280]{0:T(1024)S(1)} %broadcast_in_dim.52, f32[1280]{0:T(1024)S(1)} %broadcast_in_dim.50), kind=kLoop, calls=%fused_computation.24 | loop fusion | flops 13107200 | bytes 5263360 | tf_op jit(solution)/shard_map/convert_element_type | solution.py:44
  86.6 1.3 collective-permute-done
  87.9 4.2 %collective-permute-done.3 = bf16[1,4,1,32,1280]{4,3,2,0,1:T(8,128)(2,1)} collective-permute-done((bf16[1,4,1,32,1280]{4,3,2,0,1:T(8,128)(2,1)S(1)}, bf16[1,4,1,32,1280]{4,3,2,0,1:T(8,128)(2,1)}, u32[]{:S(2)}, u32[]{:S(2)}) %collective-permute-start.3) | collective-permute-done | bytes 327712 | tf_op jit(solution)/shard_map/ppermute | solution.py:77
  92.2 1.5 fusion.31
  93.7 0.4 maximum_bitcast_fusion.1
  94.1 2.5 copy.89
  96.6 1.6 pad.clone
  98.3 0.5 slice.23
  98.8 4.8 %fusion.1 = bf16[10,4,8,7,1280]{4,1,3,2,0:T(4,128)(2,1)} fusion(bf16[10,4,7,2,1280]{4,1,3,2,0:T(4,128)(2,1)S(1)} %slice.23, bf16[10,4,8,5,1280]{4,1,3,2,0:T(4,128)(2,1)S(1)} %bitcast.68), kind=kLoop, calls=%fused_computation.11 | loop fusion | flops 17203200 | bytes 11264000 | tf_op jit(solution)/shard_map/conv_general_dilated | solution.py:105
  103.6 4.7 %broadcast_select_fusion.1 = (bf16[2,9,1280,80]{2,3,1,0:T(8,128)(2,1)}, bf16[2,9,1280,80]{2,3,1,0:T(8,128)(2,1)}) fusion(bf16[2,9,1280,80]{2,3,1,0:T(8,128)(2,1)} %collective-permute-done.5, pred[]{:T(512)S(6)} %ne.8, bf16[1,9,1280,80]{2,3,1,0:T(8,128)(2,1)S(1)} %copy-done.1, bf16[1,9,1280,80]{2,3,1,0:T(8,128)(2,1)S(1)} %get-tuple-element.13), kind=kLoop, calls=%fused_computation.27 | loop fusion | flops 5529600 | bytes 14745601 | tf_op jit(solution)/shard_map/jit(_where)/select_n | solution.py:28
  108.3 6.8 %maximum_bitcast_fusion = bf16[9,1280,4,80]{1,3,0,2:T(8,128)(2,1)} fusion(bf16[2,9,1280,80]{2,3,1,0:T(8,128)(2,1)} %get-tuple-element.12, bf16[2,9,1280,80]{2,3,1,0:T(8,128)(2,1)} %get-tuple-element.11), kind=kLoop, calls=%fused_computation.10 | loop fusion | flops 3686400 | bytes 14745600 | tf_op jit(solution)/shard_map/transpose | solution.py:33
  115.1 3.8 %copy.75 = bf16[9,1280,4,80]{1,3,2,0:T(8,128)(2,1)S(1)} copy(bf16[9,1280,4,80]{1,3,0,2:T(8,128)(2,1)} %maximum_bitcast_fusion) | data formatting | bytes 14745600 | tf_op jit(solution)/shard_map/transpose | solution.py:33
  118.9 18.7 %select_reduce_fusion = (f32[320]{0:T(512)S(1)}, f32[320]{0:T(512)S(1)}, f32[8,32,5,320]{3,1,2,0:T(8,128)}) fusion(pred[32,5]{0,1:T(8,128)(4,1)S(1)} %copy-done.11, f32[320]{0:T(512)S(1)} %add.127, bf16[3,3,1280,320]{2,3,1,0:T(8,128)(2,1)S(1)} %bitcast.70, bf16[10,4,8,7,1280]{4,1,3,2,0:T(4,128)(2,1)} %fusion.1), kind=kOutput, calls=%fused_computation.36 | convolution fusion | flops 9440051200 | bytes 14749600 | tf_op jit(solution)/shard_map/conv_general_dilated | solution.py:105
  137.6 0.1 reduce_sum.78
  137.9 0.1 reduce_sum.81
  138.0 2.1 collective-permute-start.7
  140.1 1.3 collective-permute-done.6
  141.4 0.3 collective-permute-done.7
  142.0 2.2 multiply_convert_fusion
  144.2 0.3 copy.76
  144.6 1.6 collective-permute-start.8
  146.2 15.0 %collective-permute-done.8 = bf16[4,8,32,320]{3,1,2,0:T(8,128)(2,1)S(1)} collective-permute-done((bf16[4,8,32,320]{3,1,2,0:T(8,128)(2,1)S(1)}, bf16[4,8,32,320]{3,1,2,0:T(8,128)(2,1)S(1)}, u32[]{:S(2)}, u32[]{:S(2)}) %collective-permute-start.8) | collective-permute-done | bytes 655392 | tf_op jit(solution)/shard_map/ppermute | solution.py:152
  161.3 2.1 maximum_select_fusion.2
  163.4 2.6 collective-permute-start.9
  166.0 1.5 broadcast_select_fusion.5
  167.5 0.2 pad_maximum_fusion.1
  167.7 6.2 %copy.80 = bf16[3,1280,320]{2,0,1:T(4,128)(2,1)} copy(bf16[3,1280,320]{1,2,0:T(8,128)(2,1)S(1)} %bitcast.69) | data formatting | bytes 4915200 | tf_op jit(solution)/shard_map/reshape | solution.py:34
  173.9 12.0 %gather_fusion.3 = bf16[1280,3,320]{2,1,0:T(4,128)(2,1)} fusion(bf16[3,1280,320]{2,0,1:T(4,128)(2,1)} %copy.80, s32[2048]{0:T(1024)S(1)} %pad_clamp_fusion), kind=kCustom, calls=%fused_computation.3 | custom fusion | bytes 4920320 | tf_op jit(solution)/shard_map/gather | solution.py:160
  186.2 1.1 fusion.25
  187.3 32.4 %collective-permute-done.9 = bf16[4,8,32,640]{3,1,2,0:T(8,128)(2,1)} collective-permute-done((bf16[4,8,32,640]{3,1,2,0:T(8,128)(2,1)}, bf16[4,8,32,640]{3,1,2,0:T(8,128)(2,1)}, u32[]{:S(2)}, u32[]{:S(2)}) %collective-permute-start.9) | collective-permute-done | bytes 1310752 | tf_op jit(solution)/shard_map/ppermute | solution.py:152
  219.7 1.5 copy.79
  221.2 0.7 maximum_select_fusion
  221.9 1.4 copy-done.6
  223.3 4.4 %fusion.26 = bf16[1,4,8,32,320]{4,2,3,0,1:T(8,128)(2,1)S(1)} fusion(bf16[3,1,1280,320]{3,0,2,1:T(4,128)(2,1)S(1)} %bitcast.78, bf16[4,8,32,1280]{3,2,1,0:T(8,128)(2,1)S(1)} %bitcast.76), kind=kOutput, calls=%fused_computation.46 | convolution fusion | flops 2097479680 | bytes 5734400 | tf_op jit(solution)/shard_map/conv_general_dilated | solution.py:163
  227.7 24.8 %all_to_all.15 = bf16[1,4,8,32,320]{4,2,3,0,1:T(8,128)(2,1)S(1)} all-to-all(bf16[1,4,8,32,320]{4,2,3,0,1:T(8,128)(2,1)S(1)} %fusion.26), channel_id=1, replica_groups=mesh['rep'=4,'frame'=4,'row'=2] {'frame'}, dimensions={1} | all-to-all | bytes 1310720 | tf_op jit(solution)/shard_map/all_to_all | solution.py:172
  252.5 0.6 reshape.297
  253.2 0.4 copy.85
  253.6 0.8 gather_fusion.4
  254.3 0.3 convert_bitcast_fusion
  254.6 1.4 copy.86
  256.0 2.2 reshape.235
  258.2 2.3 add_add_fusion
  (57 shorter events, 1.9 us)
Async XLA Ops:
  6.5 65.0 %all-gather.2.cloned.1.call-start = ((), (), s32[]{:S(2)}) async-start(), calls=%async_computation.1 | async-start | bytes 3276800 | tf_op jit(solution)/shard_map/all_gather | solution.py:71
  7.3 59.1 %collective-permute-start.4 = (bf16[1,9,1280,80]{2,3,1,0:T(8,128)(2,1)}, bf16[1,9,1280,80]{2,3,1,0:T(8,128)(2,1)}, u32[]{:S(2)}, u32[]{:S(2)}) collective-permute-start(bf16[1,9,1280,80]{2,3,1,0:T(8,128)(2,1)} %bitcast.79), channel_id=1, source_target_pairs={{0,16},{8,24},{16,0},{24,8},{1,17},{9,25},{17,1},{25,9},{2,18},{10... | collective-permute-start | bytes 5529608 | tf_op jit(solution)/shard_map/ppermute | solution.py:26
  10.3 53.6 %collective-permute-start.10 = (bf16[1,3,1280,80]{2,3,0,1:T(8,128)(2,1)}, bf16[1,3,1280,80]{2,3,0,1:T(8,128)(2,1)S(1)}, u32[]{:S(2)}, u32[]{:S(2)}) collective-permute-start(bf16[1,3,1280,80]{2,3,0,1:T(8,128)(2,1)} %bitcast.80), channel_id=1, source_target_pairs={{0,16},{8,24},{16,0},{24,8},{1,17},{9,25},{17,1},{25,9},{2,18},{10... | collective-permute-start | bytes 1843208 | tf_op jit(solution)/shard_map/ppermute | solution.py:26
  65.0 1.3 copy-start.2
  66.3 99.7 %collective-permute-start.11 = (bf16[2,3,1280,80]{2,3,0,1:T(8,128)(2,1)}, bf16[2,3,1280,80]{2,3,0,1:T(8,128)(2,1)}, u32[]{:S(2)}, u32[]{:S(2)}) collective-permute-start(bf16[2,3,1280,80]{2,3,0,1:T(8,128)(2,1)} %pad_maximum_fusion.2), channel_id=1, source_target_pairs={{0,8},{8,0},{16,24},{24,16},{1,9},{9,1},{17,25},{25,17},{2,10},{10... | collective-permute-start | bytes 3686408 | tf_op jit(solution)/shard_map/ppermute | solution.py:26
  68.6 2.4 copy-start
  71.0 12.0 %copy-start.7 = (f32[1280]{0:T(1024)S(1)}, f32[1280]{0:T(1024)}, u32[]{:S(2)}) copy-start(f32[1280]{0:T(1024)} %param.23) | copy-start | bytes 15364
  71.0 12.0 %copy-start.8 = (f32[1280]{0:T(1024)S(1)}, f32[1280]{0:T(1024)}, u32[]{:S(2)}) copy-start(f32[1280]{0:T(1024)} %param.22) | copy-start | bytes 15364
  71.0 32.6 %collective-permute-start.5 = (bf16[2,9,1280,80]{2,3,1,0:T(8,128)(2,1)}, bf16[2,9,1280,80]{2,3,1,0:T(8,128)(2,1)}, u32[]{:S(2)}, u32[]{:S(2)}) collective-permute-start(bf16[2,9,1280,80]{2,3,1,0:T(8,128)(2,1)} %pad_maximum_fusion), channel_id=1, source_target_pairs={{0,8},{8,0},{16,24},{24,16},{1,9},{9,1},{17,25},{25,17},{2,10},{10... | collective-permute-start | bytes 11059208 | tf_op jit(solution)/shard_map/ppermute | solution.py:26
  74.2 7.2 %collective-permute-start.1 = (f32[1,32]{1,0:T(1,128)S(1)}, f32[1,32]{1,0:T(1,128)S(1)}, u32[]{:S(2)}, u32[]{:S(2)}) collective-permute-start(f32[1,32]{1,0:T(1,128)S(1)} %bitcast.81), channel_id=1, source_target_pairs={{0,1},{1,0},{2,3},{3,2},{4,5},{5,4},{6,7},{7,6},{8,9},{9,8},{10,11... | collective-permute-start | bytes 392 | tf_op jit(solution)/shard_map/ppermute | solution.py:13
  76.2 6.5 %collective-permute-start.2 = (f32[1,32]{1,0:T(1,128)S(1)}, f32[1,32]{1,0:T(1,128)S(1)}, u32[]{:S(2)}, u32[]{:S(2)}) collective-permute-start(f32[1,32]{1,0:T(1,128)S(1)} %bitcast.82), channel_id=1, source_target_pairs={{0,1},{1,0},{2,3},{3,2},{4,5},{5,4},{6,7},{7,6},{8,9},{9,8},{10,11... | collective-permute-start | bytes 392 | tf_op jit(solution)/shard_map/ppermute | solution.py:13
  77.7 10.3 %collective-permute-start = (bf16[1,4,1,32,1280]{4,3,2,0,1:T(8,128)(2,1)S(1)}, bf16[1,4,1,32,1280]{4,3,2,0,1:T(8,128)(2,1)S(1)}, u32[]{:S(2)}, u32[]{:S(2)}) collective-permute-start(bf16[1,4,1,32,1280]{4,3,2,0,1:T(8,128)(2,1)S(1)} %get-tuple-element.15), channel_id=1, source_target_pairs={{0,1},{2,3},{4,5},{6,7},{8,9},{10,11},{12,13},{14,15},{16,17},{18,... | collective-permute-start | bytes 983048 | tf_op jit(solution)/shard_map/ppermute | solution.py:76
  81.4 10.8 %collective-permute-start.3 = (bf16[1,4,1,32,1280]{4,3,2,0,1:T(8,128)(2,1)S(1)}, bf16[1,4,1,32,1280]{4,3,2,0,1:T(8,128)(2,1)}, u32[]{:S(2)}, u32[]{:S(2)}) collective-permute-start(bf16[1,4,1,32,1280]{4,3,2,0,1:T(8,128)(2,1)S(1)} %get-tuple-element.16), channel_id=1, source_target_pairs={{1,0},{3,2},{5,4},{7,6},{9,8},{11,10},{13,12},{15,14},{17,16},{19,... | collective-permute-start | bytes 983048 | tf_op jit(solution)/shard_map/ppermute | solution.py:77
  98.8 4.8 %copy-start.1 = (bf16[1,9,1280,80]{2,3,1,0:T(8,128)(2,1)S(1)}, bf16[1,9,1280,80]{2,3,1,0:T(8,128)(2,1)}, u32[]{:S(2)}) copy-start(bf16[1,9,1280,80]{2,3,1,0:T(8,128)(2,1)} %copy-done) | copy-start | bytes 5529604
  115.1 3.8 %copy-start.11 = (pred[32,5]{0,1:T(8,128)(4,1)S(1)}, pred[32,5]{0,1:T(8,128)(4,1)}, u32[]{:S(2)}) copy-start(pred[32,5]{0,1:T(8,128)(4,1)} %constant.73) | copy-start | bytes 484
  137.7 3.6 %collective-permute-start.6 = (f32[8]{0:T(128)S(1)}, f32[8]{0:T(128)S(1)}, u32[]{:S(2)}, u32[]{:S(2)}) collective-permute-start(f32[8]{0:T(128)S(1)} %reduce_sum.78), channel_id=1, source_target_pairs={{0,1},{1,0},{2,3},{3,2},{4,5},{5,4},{6,7},{7,6},{8,9},{9,8},{10,11... | collective-permute-start | bytes 104 | tf_op jit(solution)/shard_map/ppermute | solution.py:13
  138.0 3.6 %collective-permute-start.7 = (f32[8]{0:T(128)S(1)}, f32[8]{0:T(128)S(1)}, u32[]{:S(2)}, u32[]{:S(2)}) collective-permute-start(f32[8]{0:T(128)S(1)} %reduce_sum.81), channel_id=1, source_target_pairs={{0,1},{1,0},{2,3},{3,2},{4,5},{5,4},{6,7},{7,6},{8,9},{9,8},{10,11... | collective-permute-start | bytes 104 | tf_op jit(solution)/shard_map/ppermute | solution.py:13
  144.5 21.5 %copy-start.10 = (s32[1280]{0:T(1024)S(1)}, s32[1280]{0:T(1024)}, u32[]{:S(2)}) copy-start(s32[1280]{0:T(1024)} %constant.82) | copy-start | bytes 15364
  144.5 21.5 %copy-start.3 = (bf16[1,3,1280,80]{2,3,0,1:T(8,128)(2,1)S(1)}, bf16[1,3,1280,80]{2,3,0,1:T(8,128)(2,1)}, u32[]{:S(2)}) copy-start(bf16[1,3,1280,80]{2,3,0,1:T(8,128)(2,1)} %copy-done.2) | copy-start | bytes 1843204
  144.6 16.7 %collective-permute-start.8 = (bf16[4,8,32,320]{3,1,2,0:T(8,128)(2,1)S(1)}, bf16[4,8,32,320]{3,1,2,0:T(8,128)(2,1)S(1)}, u32[]{:S(2)}, u32[]{:S(2)}) collective-permute-start(bf16[4,8,32,320]{3,1,2,0:T(8,128)(2,1)S(1)} %slice_bitcast_fusion), channel_id=1, source_target_pairs={{0,2},{2,0},{4,6},{6,4},{1,3},{3,1},{5,7},{7,5},{8,10},{10,8},{12,... | collective-permute-start | bytes 1966088 | tf_op jit(solution)/shard_map/ppermute | solution.py:152
  161.3 6.2 %copy-start.4 = (bf16[4,8,32,320]{3,1,2,0:T(8,128)(2,1)}, bf16[4,8,32,320]{3,1,2,0:T(8,128)(2,1)S(1)}, u32[]{:S(2)}) copy-start(bf16[4,8,32,320]{3,1,2,0:T(8,128)(2,1)S(1)} %collective-permute-done.8) | copy-start | bytes 1966084
  163.4 56.3 %collective-permute-start.9 = (bf16[4,8,32,640]{3,1,2,0:T(8,128)(2,1)}, bf16[4,8,32,640]{3,1,2,0:T(8,128)(2,1)}, u32[]{:S(2)}, u32[]{:S(2)}) collective-permute-start(bf16[4,8,32,640]{3,1,2,0:T(8,128)(2,1)} %maximum_select_fusion.2), channel_id=1, source_target_pairs={{0,4},{2,6},{4,0},{6,2},{1,5},{3,7},{5,1},{7,3},{8,12},{10,14},{12... | collective-permute-start | bytes 3932168 | tf_op jit(solution)/shard_map/ppermute | solution.py:152
  173.9 12.2 %copy-start.5 = (bf16[4,8,32,320]{3,1,2,0:T(8,128)(2,1)S(1)}, bf16[4,8,32,320]{3,1,2,0:T(8,128)(2,1)}, u32[]{:S(2)}) copy-start(bf16[4,8,32,320]{3,1,2,0:T(8,128)(2,1)} %copy-done.4) | copy-start | bytes 1966084
  221.2 2.1 copy-start.6
  256.0 2.3 copy-start.9
Sparse Core Ops, SparseCore 0:
  8.9 57.4 all-gather.1
